TPU v7x, 256 devices: a whole 4x4x8 slice. The times are simulated.
256 devices in a mesh: row: 32 (over y, x, core), col: 8 (over z).
Axes of the slice: x: 4, y: 4, z: 8, core: 2. Of those that a mesh axis runs over, the one named last changes fastest.
Arguments:
- covariance: float32 [8192, 8192], P('row', 'col'), may hold values from 0 to 4, as said below
- panels: int32 [4], replicated, may hold values from 0 to 31, as said below
- observed: float32 [8192], P('row'), may hold values from -6 to 6
- drift_basis: float32 [64, 8192], P(None, 'row'), may hold values from -1.5 to 1.5
Outputs:
- complement: float32 [8192, 8192], P('row', 'col')
- factor: float32 [8192, 1024], P('row')
- solved_data: float32 [8192], P('row')
- solved_drift: float32 [64, 8192], P(None, 'row')
Inputs may be any that keep to these rules, and one draw needn't show every extreme that they name: `covariance`: symmetric and positive definite. `panels`: 4 different tile indices; tile 32 - 1 is always among them.
All inputs are finite; a program needn't handle non-finite values.
Results may differ from a plain program's by a relative error of at most 0.0003.
Values sent between devices are 32-bit elements; how exact they have to be, the bound alone decides.
No kernel may reach another device: no remote copies, remote signals or barrier semaphores. Data moves between devices by JAX's collectives and lax.ppermute only.
A program may use at most 64 MiB of HBM per device.

v0:
```python
import jax
import jax.numpy as jnp
from jax import lax
from jax.sharding import PartitionSpec as P

B = 256
K = 4


def from_root(value, axis, root):
    return lax.dynamic_index_in_dim(lax.all_gather(value, axis), root, 0, keepdims=False)


def broadcast(value, axis, root):
    mine = lax.axis_index(axis) == root
    return lax.psum(jnp.where(mine, value, jnp.zeros_like(value)), axis)


def solve_right(chol_tile, values):
    return lax.linalg.triangular_solve(
        chol_tile, values, left_side=False, lower=True, transpose_a=True
    )


def keep_mask(tiles, chosen):
    return jnp.all(tiles[:, None] != chosen[None, :], axis=1).astype(jnp.float32)


def outer_product(rows_factor, cols_factor):
    return lax.dot_general(
        rows_factor, cols_factor, (((1,), (0,)), ((), ())), precision=lax.Precision.HIGHEST
    )


def on_device(covariance, panels, observed, drift_basis):
    rows_here = covariance.shape[0]
    cols_here = covariance.shape[1]
    row_start = lax.axis_index("row") * rows_here
    col_start = lax.axis_index("col") * cols_here
    row_tiles = (row_start + lax.iota(jnp.int32, rows_here)) // B
    col_tiles = (col_start + lax.iota(jnp.int32, cols_here)) // B
    sides = jnp.concatenate([observed[None, :], drift_basis], axis=0)
    matrix = covariance
    factors = []
    for position in range(K):
        target = panels[position]
        offset = target * B
        row_owner = offset // rows_here
        col_owner = offset // cols_here
        col_off = offset - col_owner * cols_here
        keep_rows = keep_mask(row_tiles, panels[:position])
        keep_cols = keep_mask(col_tiles, panels[:position])
        col_slab = lax.dynamic_slice_in_dim(matrix, col_off, B, 1)
        col_slab = from_root(col_slab, "col", col_owner)
        side_tile = sides
        diag_tile = col_slab
        row_slab = matrix
        row_slab, diag_tile, side_tile = (
            broadcast(row_slab, "row", row_owner),
            broadcast(diag_tile, "row", row_owner),
            broadcast(side_tile, "row", row_owner),
        )
        chol_tile = jnp.linalg.cholesky(diag_tile)
        rows_factor = solve_right(chol_tile, col_slab) * keep_rows[:, None]
        cols_factor = (
            lax.linalg.triangular_solve(
                chol_tile, row_slab, left_side=True, lower=True, transpose_a=False
            )
            * keep_cols[None, :]
        )
        solved = solve_right(chol_tile, side_tile)
        matrix = matrix - outer_product(rows_factor, cols_factor)
        sides = sides - lax.dot_general(
            solved, rows_factor, (((1,), (1,)), ((), ())), precision=lax.Precision.HIGHEST
        )
        sides = jnp.where((row_tiles == target)[None, :], solved, sides)
        factors.append(rows_factor)
    final_rows = keep_mask(row_tiles, panels)
    final_cols = keep_mask(col_tiles, panels)
    complement = matrix * final_rows[:, None] * final_cols[None, :]
    return (complement, jnp.concatenate(factors, axis=1), sides[0], sides[1:])


def solution(mesh):
    return jax.shard_map(
        on_device,
        mesh=mesh,
        in_specs=(P("row", "col"), P(), P("row"), P(None, "row")),
        out_specs=(P("row", "col"), P("row", None), P("row"), P(None, "row")),
        check_vma=False,
    )
```

profile of v0, /device:TPU:6, one launch (start us, length us, event | category | flops | bytes accessed | tf_op | source)
XLA Modules:
  0.0 943.6 jit_solution(15376847191350219697)
XLA Ops:
  7.2 1.4 fusion.110
  9.3 1.7 constant_dynamic-slice_fusion.11
  11.1 1.5 fusion.62
  12.6 1.1 broadcast_select_fusion.3
  13.6 41.5 %all-gather.9.cloned.1.call-done = f32[2048,256]{1,0:T(8,128)} async-done(((f32[256,256]{1,0:T(8,128)}), f32[2048,256]{1,0:T(8,128)}) %all-gather.9.cloned.1.call-update) | async-done | bytes 2097168 | tf_op jit(solution)/shard_map/all_gather | solution.py:11
  55.2 1.0 constant_dynamic-slice_fusion.10
  57.8 117.0 %all-reduce.16.cloned.1.call-done = (f32[256,1024]{1,0:T(8,128)}, f32[256,256]{0,1:T(8,128)}, f32[65,256]{1,0:T(8,128)}) async-done(((f32[256,1024]{1,0:T(8,128)}, f32[256,256]{0,1:T(8,128)}, f32[65,256]{1,0:T(8,128)}), (f32[256,1024]{1,0:T(8,128)}, f32[256,256]{0,1:T(8,128)}, f32[65,256]{1,0:T(8,128)})) %all-reduce.16.cloned.1.call-update) | async-done | bytes 1377296 | tf_op jit(solution)/shard_map/psum | solution.py:16
  174.8 1.1 copy.18
  175.9 1.0 fusion.29
  176.9 11.7 %cholesky.214 = f32[128,128]{1,0:T(8,128)S(1)} custom-call(f32[128,128]{1,0:T(8,128)S(1)} %cholesky.346), custom_call_target="Cholesky" | custom-call | tf_op jit(solution)/shard_map/jit(cholesky)/cholesky | solution.py:63
  188.6 9.8 %custom-call.29 = f32[1,128,128]{1,2,0:T(8,128)S(1)} custom-call(f32[1,128,128]{2,1,0:T(8,128)S(1)} %get-tuple-element.173), custom_call_target="InvertDiagBlocksLowerTriangular" | custom-call | tf_op jit(solution)/shard_map/jit(cholesky)/cholesky | solution.py:63
  198.9 11.7 %cholesky.231 = f32[128,128]{1,0:T(8,128)S(1)} custom-call(f32[128,128]{1,0:T(8,128)S(1)} %convolution_subtract_fusion.19), custom_call_target="Cholesky" | custom-call | tf_op jit(solution)/shard_map/jit(cholesky)/cholesky | solution.py:63
  212.8 4.2 while.24
  213.6 1.4 bitcast_dynamic-update-slice_fusion.8
  215.6 1.4 bitcast_dynamic-update-slice_fusion.8
  217.0 19.7 %custom-call.30 = f32[2,128,128]{1,2,0:T(8,128)S(1)} custom-call(f32[2,128,128]{2,1,0:T(8,128)S(1)} %get-tuple-element.86), custom_call_target="InvertDiagBlocksLowerTriangular" | custom-call | tf_op jit(solution)/shard_map/triangular_solve/custom-call.0 | solution.py:20
  238.2 1.6 convolution_subtract_fusion.7
  240.5 2.1 broadcast_select_fusion.2
  245.7 37.7 %all-gather.11.cloned.1.call-done = f32[2048,256]{1,0:T(8,128)} async-done(((f32[256,256]{1,0:T(8,128)}), f32[2048,256]{1,0:T(8,128)}) %all-gather.11.cloned.1.call-update) | async-done | bytes 2097168 | tf_op jit(solution)/shard_map/all_gather | solution.py:11
  283.4 1.0 constant_dynamic-slice_fusion.8
  286.2 1.3 compare_convert_fusion.1
  288.2 114.5 %all-reduce.14.cloned.1.call-done = (f32[256,256]{0,1:T(8,128)}, f32[256,1024]{1,0:T(8,128)}, f32[65,256]{1,0:T(8,128)}) async-done(((f32[256,256]{0,1:T(8,128)}, f32[256,1024]{1,0:T(8,128)}, f32[65,256]{1,0:T(8,128)}), (f32[256,256]{0,1:T(8,128)}, f32[256,1024]{1,0:T(8,128)}, f32[65,256]{1,0:T(8,128)})) %all-reduce.14.cloned.1.call-update) | async-done | bytes 1377296 | tf_op jit(solution)/shard_map/psum | solution.py:16
  402.7 1.1 copy.20
  403.8 1.0 fusion.28
  404.8 11.7 %cholesky.248 = f32[128,128]{1,0:T(8,128)S(1)} custom-call(f32[128,128]{1,0:T(8,128)S(1)} %cholesky.349), custom_call_target="Cholesky" | custom-call | tf_op jit(solution)/shard_map/jit(cholesky)/cholesky | solution.py:63
  416.6 9.8 %custom-call.32 = f32[1,128,128]{1,2,0:T(8,128)S(1)} custom-call(f32[1,128,128]{2,1,0:T(8,128)S(1)} %get-tuple-element.169), custom_call_target="InvertDiagBlocksLowerTriangular" | custom-call | tf_op jit(solution)/shard_map/jit(cholesky)/cholesky | solution.py:63
  426.9 11.7 %cholesky.265 = f32[128,128]{1,0:T(8,128)S(1)} custom-call(f32[128,128]{1,0:T(8,128)S(1)} %convolution_subtract_fusion.18), custom_call_target="Cholesky" | custom-call | tf_op jit(solution)/shard_map/jit(cholesky)/cholesky | solution.py:63
  441.3 4.5 while.25
  442.3 1.4 bitcast_dynamic-update-slice_fusion.9
  444.3 1.4 bitcast_dynamic-update-slice_fusion.9
  445.7 19.7 %custom-call.33 = f32[2,128,128]{1,2,0:T(8,128)S(1)} custom-call(f32[2,128,128]{2,1,0:T(8,128)S(1)} %get-tuple-element.88), custom_call_target="InvertDiagBlocksLowerTriangular" | custom-call | tf_op jit(solution)/shard_map/triangular_solve/custom-call.0 | solution.py:20
  466.4 1.7 fusion.19
  468.0 1.6 convolution_subtract_fusion.6
  470.3 2.1 broadcast_select_fusion.1
  474.9 38.3 %all-gather.13.cloned.1.call-done = f32[2048,256]{1,0:T(8,128)} async-done(((f32[256,256]{1,0:T(8,128)}), f32[2048,256]{1,0:T(8,128)}) %all-gather.13.cloned.1.call-update) | async-done | bytes 2097168 | tf_op jit(solution)/shard_map/all_gather | solution.py:11
  513.2 1.0 constant_dynamic-slice_fusion.6
  516.7 115.8 %all-reduce.12.cloned.1.call-done = (f32[256,256]{0,1:T(8,128)}, f32[256,1024]{1,0:T(8,128)}, f32[65,256]{1,0:T(8,128)}) async-done(((f32[256,256]{0,1:T(8,128)}, f32[256,1024]{1,0:T(8,128)}, f32[65,256]{1,0:T(8,128)}), (f32[256,256]{0,1:T(8,128)}, f32[256,1024]{1,0:T(8,128)}, f32[65,256]{1,0:T(8,128)})) %all-reduce.12.cloned.1.call-update) | async-done | bytes 1377296 | tf_op jit(solution)/shard_map/psum | solution.py:16
  632.5 1.1 copy.22
  633.6 1.0 fusion.27
  634.6 11.7 %cholesky.282 = f32[128,128]{1,0:T(8,128)S(1)} custom-call(f32[128,128]{1,0:T(8,128)S(1)} %cholesky.352), custom_call_target="Cholesky" | custom-call | tf_op jit(solution)/shard_map/jit(cholesky)/cholesky | solution.py:63
  646.9 9.8 %custom-call.35 = f32[1,128,128]{1,2,0:T(8,128)S(1)} custom-call(f32[1,128,128]{2,1,0:T(8,128)S(1)} %get-tuple-element.165), custom_call_target="InvertDiagBlocksLowerTriangular" | custom-call | tf_op jit(solution)/shard_map/jit(cholesky)/cholesky | solution.py:63
  657.2 11.7 %cholesky.299 = f32[128,128]{1,0:T(8,128)S(1)} custom-call(f32[128,128]{1,0:T(8,128)S(1)} %convolution_subtract_fusion.17), custom_call_target="Cholesky" | custom-call | tf_op jit(solution)/shard_map/jit(cholesky)/cholesky | solution.py:63
  669.6 1.3 compare_reduce_fusion.9
  672.2 5.6 while.26
  673.7 1.4 bitcast_dynamic-update-slice_fusion.10
  676.4 1.4 bitcast_dynamic-update-slice_fusion.10
  677.8 19.7 %custom-call.36 = f32[2,128,128]{1,2,0:T(8,128)S(1)} custom-call(f32[2,128,128]{2,1,0:T(8,128)S(1)} %get-tuple-element.90), custom_call_target="InvertDiagBlocksLowerTriangular" | custom-call | tf_op jit(solution)/shard_map/triangular_solve/custom-call.0 | solution.py:20
  700.3 2.1 broadcast_select_fusion
  705.5 37.7 %all-gather.15.cloned.1.call-done = f32[2048,256]{1,0:T(8,128)} async-done(((f32[256,256]{1,0:T(8,128)}), f32[2048,256]{1,0:T(8,128)}) %all-gather.15.cloned.1.call-update) | async-done | bytes 2097168 | tf_op jit(solution)/shard_map/all_gather | solution.py:11
  746.0 1.1 broadcast_compare_fusion.2
  747.1 115.5 %all-reduce.10.cloned.1.call-done = (f32[256,256]{0,1:T(8,128)}, f32[256,1024]{1,0:T(8,128)}, f32[65,256]{1,0:T(8,128)}) async-done(((f32[256,256]{0,1:T(8,128)}, f32[256,1024]{1,0:T(8,128)}, f32[65,256]{1,0:T(8,128)}), (f32[256,256]{0,1:T(8,128)}, f32[256,1024]{1,0:T(8,128)}, f32[65,256]{1,0:T(8,128)})) %all-reduce.10.cloned.1.call-update) | async-done | bytes 1377296 | tf_op jit(solution)/shard_map/psum | solution.py:16
  862.7 1.1 copy.24
  863.8 1.0 fusion.26
  864.8 11.7 %cholesky.316 = f32[128,128]{1,0:T(8,128)S(1)} custom-call(f32[128,128]{1,0:T(8,128)S(1)} %cholesky.355), custom_call_target="Cholesky" | custom-call | tf_op jit(solution)/shard_map/jit(cholesky)/cholesky | solution.py:63
  876.6 9.8 %custom-call.38 = f32[1,128,128]{1,2,0:T(8,128)S(1)} custom-call(f32[1,128,128]{2,1,0:T(8,128)S(1)} %get-tuple-element.161), custom_call_target="InvertDiagBlocksLowerTriangular" | custom-call | tf_op jit(solution)/shard_map/jit(cholesky)/cholesky | solution.py:63
  886.9 11.7 %cholesky.333 = f32[128,128]{1,0:T(8,128)S(1)} custom-call(f32[128,128]{1,0:T(8,128)S(1)} %convolution_subtract_fusion.16), custom_call_target="Cholesky" | custom-call | tf_op jit(solution)/shard_map/jit(cholesky)/cholesky | solution.py:63
  901.2 4.3 while.27
  902.1 1.4 bitcast_dynamic-update-slice_fusion.11
  904.1 1.4 bitcast_dynamic-update-slice_fusion.11
  905.5 19.7 %custom-call.39 = f32[2,128,128]{1,2,0:T(8,128)S(1)} custom-call(f32[2,128,128]{2,1,0:T(8,128)S(1)} %get-tuple-element.92), custom_call_target="InvertDiagBlocksLowerTriangular" | custom-call | tf_op jit(solution)/shard_map/triangular_solve/custom-call.0 | solution.py:20
  929.0 1.3 copy.25
  930.3 1.7 fusion.15
  932.0 1.6 convolution_subtract_fusion.4
  934.3 2.1 fusion.1
  (172 shorter events, 39.8 us)
Async XLA Ops:
  7.2 48.0 %all-gather.9.cloned.1.call-start = ((), (), s32[]{:S(2)}) async-start(), calls=%async_computation | async-start | bytes 2359296 | tf_op jit(solution)/shard_map/all_gather | solution.py:11
  11.0 163.8 %all-reduce.16.cloned.1.call-start = ((), (), s32[]{:S(2)}) async-start(), calls=%async_computation.7 | async-start | bytes 2768896 | tf_op jit(solution)/shard_map/psum | solution.py:16
  57.0 226.4 %all-gather.11.cloned.1.call-start = ((), (), s32[]{:S(2)}) async-start(), calls=%async_computation.1 | async-start | bytes 2359296 | tf_op jit(solution)/shard_map/all_gather | solution.py:11
  176.8 60.7 %copy-start.2 = (f32[256,1024]{1,0:T(8,128)S(1)}, f32[256,1024]{1,0:T(8,128)}, u32[]{:S(2)}) copy-start(f32[256,1024]{1,0:T(8,128)} %get-tuple-element.147) | copy-start | bytes 3145732
  237.3 3.3 copy-start
  240.5 3.6 copy-start.7
  240.5 4.3 copy-start.4
  240.5 4.3 copy-start.10
  243.3 159.4 %all-reduce.14.cloned.1.call-start = ((), (), s32[]{:S(2)}) async-start(), calls=%async_computation.6 | async-start | bytes 2768896 | tf_op jit(solution)/shard_map/psum | solution.py:16
  285.3 227.9 %all-gather.13.cloned.1.call-start = ((), (), s32[]{:S(2)}) async-start(), calls=%async_computation.2 | async-start | bytes 2359296 | tf_op jit(solution)/shard_map/all_gather | solution.py:11
  445.7 20.6 %copy-start.13 = (s32[2,2]{1,0:T(2,128)}, s32[2,2]{1,0:T(2,128)S(1)}, u32[]{:S(2)}) copy-start(s32[2,2]{1,0:T(2,128)S(1)} %get-tuple-element.455) | copy-start | bytes 52
  470.3 2.9 copy-start.6
  473.1 42.7 %copy-start.9 = (s32[4]{0:T(128)S(1)}, s32[4]{0:T(128)}, u32[]{:S(2)}) copy-start(s32[4]{0:T(128)} %param.12) | copy-start | bytes 52
  473.1 159.4 %all-reduce.12.cloned.1.call-start = ((), (), s32[]{:S(2)}) async-start(), calls=%async_computation.5 | async-start | bytes 2768896 | tf_op jit(solution)/shard_map/psum | solution.py:16
  515.0 228.2 %all-gather.15.cloned.1.call-start = ((), (), s32[]{:S(2)}) async-start(), calls=%async_computation.3 | async-start | bytes 2359296 | tf_op jit(solution)/shard_map/all_gather | solution.py:11
  634.6 63.8 %copy-start.1 = (f32[256,1024]{1,0:T(8,128)S(1)}, f32[256,1024]{1,0:T(8,128)}, u32[]{:S(2)}) copy-start(f32[256,1024]{1,0:T(8,128)} %get-tuple-element.142) | copy-start | bytes 3145732
  698.1 2.2 copy-start.11
  700.3 3.5 copy-start.5
  700.3 4.2 copy-start.3
  703.1 159.5 %all-reduce.10.cloned.1.call-start = ((), (), s32[]{:S(2)}) async-start(), calls=%async_computation.4 | async-start | bytes 2768896 | tf_op jit(solution)/shard_map/psum | solution.py:16
  745.0 156.2 %copy-start.14 = (s32[2,2]{1,0:T(2,128)S(1)}, s32[2,2]{1,0:T(2,128)}, u32[]{:S(2)}) copy-start(s32[2,2]{1,0:T(2,128)} %get-tuple-element.456) | copy-start | bytes 52
  862.7 62.5 %copy-start.8 = (f32[65,256]{1,0:T(8,128)S(1)}, f32[65,256]{1,0:T(8,128)}, u32[]{:S(2)}) copy-start(f32[65,256]{1,0:T(8,128)} %get-tuple-element.140) | copy-start | bytes 199684
  876.5 50.3 %copy-start.12 = (f32[256]{0:T(256)S(1)}, f32[256]{0:T(256)}, u32[]{:S(2)}) copy-start(f32[256]{0:T(256)} %convert_element_type.60) | copy-start | bytes 3076
Sparse Core Ops, SparseCore 0:
  11.1 44.0 all-gather.8
  59.4 115.3 all-reduce.15
  243.5 39.8 all-gather.10
  287.5 115.1 all-reduce.13
  473.2 39.8 all-gather.12
  517.3 115.1 all-reduce.11
  703.3 39.8 all-gather.14
  747.4 115.1 all-reduce.9
where the time goes:
time: 953 us; the launch traced here: 944 us
  waiting for transfers between devices  618 us (65%)
  other arithmetic  233 us (24%)
  local copies, waits for them, and re-layouts  33.9 us (4%)
  matrix products  32.6 us (3%)
  between operations  23.3 us (2%)
    psum x4, waiting for transfers between devices, broadcast(): return lax.psum(jnp.where(mine, value, jnp.zeros_like(value)), axis)  463 us
    all_gather x4, waiting for transfers between devices, from_root(): lax.all_gather(value, axis)  155 us
    another operation x27, other arithmetic, on_device(): chol_tile = jnp.linalg.cholesky(diag_tile)  139 us
    another operation x9, other arithmetic, solve_right(): lax.linalg.triangular_solve(chol_tile, values, left_side=False, lower=Tru...  78.8 us
  transfers between devices with their start and end apart: 8, of which 8 were waited for; matrix products, arithmetic and copies ran while one was open for 1% of the time, Pallas kernels for 0%

commit v1 on v0

--- a/solution.py
+++ b/solution.py
@@ -7,13 +7,19 @@
 K = 4
 
 
+def add_all(x, name):
+    shards = lax.all_gather(x, name, axis=0, tiled=False)
+    result = shards.sum(axis=0)
+    return result
+
+
 def from_root(value, axis, root):
     return lax.dynamic_index_in_dim(lax.all_gather(value, axis), root, 0, keepdims=False)
 
 
 def broadcast(value, axis, root):
     mine = lax.axis_index(axis) == root
-    return lax.psum(jnp.where(mine, value, jnp.zeros_like(value)), axis)
+    return add_all(jnp.where(mine, value, jnp.zeros_like(value)), axis)
 
 
 def solve_right(chol_tile, values):

time: 953 us -> 1160 us (1.22)
  waiting for transfers between devices: 618 us -> 770 us
  other arithmetic: 233 us -> 303 us
    all_gather x0 -> x12, waiting for transfers between devices: none -> 605 us  [add_all(): shards = lax.all_gather(x, name, axis=0, tiled=False)]
    psum x4 -> x0, waiting for transfers between devices: 463 us -> none  [broadcast(): return lax.psum(jnp.where(mine, value, jnp.zeros_like(value)), axis)]
    reduce_sum x0 -> x12, other arithmetic: none -> 70.4 us  [add_all(): result = shards.sum(axis=0)]
  transfers between devices with their start and end apart: 8 -> 16, of which waited for: 8 -> 16; matrix products, arithmetic and copies ran while one was open for 1% -> 28% of each run, Pallas kernels for 0% -> 0%
where the time goes in v1:
time: 1160 us; the launch traced here: 1150 us
  waiting for transfers between devices  770 us (66%)
  other arithmetic  303 us (26%)
  matrix products  27.9 us (2%)
  local copies, waits for them, and re-layouts  24.4 us (2%)
  between operations  23.1 us (2%)
    all_gather x12, waiting for transfers between devices, add_all(): shards = lax.all_gather(x, name, axis=0, tiled=False)  605 us
    all_gather x4, waiting for transfers between devices, from_root(): lax.all_gather(value, axis)  163 us
    another operation x27, other arithmetic, on_device(): chol_tile = jnp.linalg.cholesky(diag_tile)  138 us
    another operation x9, other arithmetic, solve_right(): lax.linalg.triangular_solve(chol_tile, values, left_side=False, lower=Tru...  78.8 us
    reduce_sum x12, other arithmetic, add_all(): result = shards.sum(axis=0)  70.4 us
  transfers between devices with their start and end apart: 16, of which 16 were waited for; matrix products, arithmetic and copies ran while one was open for 28% of the time, Pallas kernels for 0%

profile of v1, /device:TPU:6, one launch (start us, length us, event | category | flops | bytes accessed | tf_op | source)
XLA Modules:
  0.0 1150.4 jit_solution(55648069791971921)
XLA Ops:
  7.2 1.5 fusion.109
  9.3 1.7 constant_dynamic-slice_fusion.7
  11.1 44.1 %all-gather.41.cloned.1.call-done = f32[2048,256]{1,0:T(8,128)} async-done(((f32[256,256]{1,0:T(8,128)}), f32[2048,256]{1,0:T(8,128)}) %all-gather.41.cloned.1.call-update) | async-done | bytes 2097168 | tf_op jit(solution)/shard_map/all_gather | solution.py:17
  55.2 1.7 dynamic-slice_bitcast_fusion.3
  58.7 56.1 %all-gather.31.cloned.1.call-done = f32[32,256,256]{2,1,0:T(8,128)} async-done(((f32[1,256,256]{2,1,0:T(8,128)}), f32[32,256,256]{2,1,0:T(8,128)}) %all-gather.31.cloned.1.call-update) | async-done | bytes 8388624 | tf_op jit(solution)/shard_map/all_gather | solution.py:11
  114.8 3.9 reduce_sum.108
  118.9 11.7 %cholesky.214 = f32[128,128]{1,0:T(8,128)S(1)} custom-call(f32[128,128]{1,0:T(8,128)S(1)} %cholesky.346), custom_call_target="Cholesky" | custom-call | tf_op jit(solution)/shard_map/jit(cholesky)/cholesky | solution.py:69
  130.6 9.8 custom-call.29
  141.0 11.7 %cholesky.231 = f32[128,128]{1,0:T(8,128)S(1)} custom-call(f32[128,128]{1,0:T(8,128)S(1)} %convolution_subtract_fusion.19), custom_call_target="Cholesky" | custom-call | tf_op jit(solution)/shard_map/jit(cholesky)/cholesky | solution.py:69
  154.9 4.3 while.24
  155.7 1.4 bitcast_dynamic-update-slice_fusion.8
  157.7 1.4 bitcast_dynamic-update-slice_fusion.8
  159.2 19.7 %custom-call.30 = f32[2,128,128]{1,2,0:T(8,128)S(1)} custom-call(f32[2,128,128]{2,1,0:T(8,128)S(1)} %get-tuple-element.86), custom_call_target="InvertDiagBlocksLowerTriangular" | custom-call | tf_op jit(solution)/shard_map/triangular_solve/custom-call.0 | solution.py:26
  179.9 56.7 %all-gather.43.cloned.1.call-done = f32[8192,1024]{1,0:T(8,128)} async-done(((f32[256,1024]{1,0:T(8,128)}), f32[8192,1024]{1,0:T(8,128)}) %all-gather.43.cloned.1.call-update) | async-done | bytes 33554448 | tf_op jit(solution)/shard_map/all_gather | solution.py:11
  236.7 11.8 %reduce_sum.109 = f32[256,1024]{1,0:T(8,128)S(1)} reduce(f32[32,256,1024]{2,1,0:T(8,128)} %bitcast.244, f32[]{:T(128)} %constant.178.clone.1), dimensions={0}, to_apply=%region_5.8 | reduce | flops 8126464 | bytes 34603012 | tf_op jit(solution)/shard_map/reduce_sum | solution.py:12
  250.4 2.0 broadcast_select_fusion.2
  253.3 40.5 %all-gather.45.cloned.1.call-done = f32[2048,256]{1,0:T(8,128)} async-done(((f32[256,256]{1,0:T(8,128)}), f32[2048,256]{1,0:T(8,128)}) %all-gather.45.cloned.1.call-update) | async-done | bytes 2097168 | tf_op jit(solution)/shard_map/all_gather | solution.py:17
  293.8 1.7 dynamic-slice_select_fusion.2
  298.7 54.5 %all-gather.33.cloned.1.call-done = f32[32,256,256]{2,1,0:T(8,128)} async-done(((f32[1,256,256]{2,1,0:T(8,128)}), f32[32,256,256]{2,1,0:T(8,128)}) %all-gather.33.cloned.1.call-update) | async-done | bytes 8388624 | tf_op jit(solution)/shard_map/all_gather | solution.py:11
  353.2 3.9 reduce_sum.110
  357.3 11.7 %cholesky.248 = f32[128,128]{1,0:T(8,128)S(1)} custom-call(f32[128,128]{1,0:T(8,128)S(1)} %cholesky.349), custom_call_target="Cholesky" | custom-call | tf_op jit(solution)/shard_map/jit(cholesky)/cholesky | solution.py:69
  369.1 9.8 custom-call.32
  379.4 11.7 %cholesky.265 = f32[128,128]{1,0:T(8,128)S(1)} custom-call(f32[128,128]{1,0:T(8,128)S(1)} %convolution_subtract_fusion.18), custom_call_target="Cholesky" | custom-call | tf_op jit(solution)/shard_map/jit(cholesky)/cholesky | solution.py:69
  393.7 4.2 while.25
  397.9 19.7 %custom-call.33 = f32[2,128,128]{1,2,0:T(8,128)S(1)} custom-call(f32[2,128,128]{2,1,0:T(8,128)S(1)} %get-tuple-element.88), custom_call_target="InvertDiagBlocksLowerTriangular" | custom-call | tf_op jit(solution)/shard_map/triangular_solve/custom-call.0 | solution.py:26
  418.7 56.2 %all-gather.47.cloned.1.call-done = f32[8192,1024]{1,0:T(8,128)} async-done(((f32[256,1024]{1,0:T(8,128)}), f32[8192,1024]{1,0:T(8,128)}) %all-gather.47.cloned.1.call-update) | async-done | bytes 33554448 | tf_op jit(solution)/shard_map/all_gather | solution.py:11
  474.8 11.8 %reduce_sum.111 = f32[256,1024]{1,0:T(8,128)S(1)} reduce(f32[32,256,1024]{2,1,0:T(8,128)} %bitcast.243, f32[]{:T(128)} %constant.178.clone.1), dimensions={0}, to_apply=%region_7.11 | reduce | flops 8126464 | bytes 34603012 | tf_op jit(solution)/shard_map/reduce_sum | solution.py:12
  488.6 2.0 broadcast_select_fusion.1
  492.0 33.8 %all-gather.39.cloned.1.call-done = f32[32,65,256]{2,1,0:T(8,128)} async-done(((f32[1,65,256]{2,1,0:T(8,128)}), f32[32,65,256]{2,1,0:T(8,128)}) %all-gather.39.cloned.1.call-update) | async-done | bytes 2129936 | tf_op jit(solution)/shard_map/all_gather | solution.py:11
  525.8 1.8 reduce_sum.116
  530.2 38.9 %all-gather.49.cloned.1.call-done = f32[2048,256]{1,0:T(8,128)} async-done(((f32[256,256]{1,0:T(8,128)}), f32[2048,256]{1,0:T(8,128)}) %all-gather.49.cloned.1.call-update) | async-done | bytes 2097168 | tf_op jit(solution)/shard_map/all_gather | solution.py:17
  569.1 1.7 dynamic-slice_select_fusion.1
  573.1 46.0 %all-gather.57.cloned.1.call-done = f32[32,65,256]{2,1,0:T(8,128)} async-done(((f32[1,65,256]{2,1,0:T(8,128)}), f32[32,65,256]{2,1,0:T(8,128)}) %all-gather.57.cloned.1.call-update) | async-done | bytes 2129936 | tf_op jit(solution)/shard_map/all_gather | solution.py:11
  619.1 1.8 reduce_sum.117
  623.6 56.1 %all-gather.35.cloned.1.call-done = f32[32,256,256]{2,1,0:T(8,128)} async-done(((f32[1,256,256]{2,1,0:T(8,128)}), f32[32,256,256]{2,1,0:T(8,128)}) %all-gather.35.cloned.1.call-update) | async-done | bytes 8388624 | tf_op jit(solution)/shard_map/all_gather | solution.py:11
  679.8 3.9 reduce_sum.112
  683.9 11.7 %cholesky.282 = f32[128,128]{1,0:T(8,128)S(1)} custom-call(f32[128,128]{1,0:T(8,128)S(1)} %cholesky.352), custom_call_target="Cholesky" | custom-call | tf_op jit(solution)/shard_map/jit(cholesky)/cholesky | solution.py:69
  695.7 9.8 custom-call.35
  706.0 11.7 %cholesky.299 = f32[128,128]{1,0:T(8,128)S(1)} custom-call(f32[128,128]{1,0:T(8,128)S(1)} %convolution_subtract_fusion.17), custom_call_target="Cholesky" | custom-call | tf_op jit(solution)/shard_map/jit(cholesky)/cholesky | solution.py:69
  720.5 4.3 while.26
  721.3 1.4 bitcast_dynamic-update-slice_fusion.10
  723.3 1.4 bitcast_dynamic-update-slice_fusion.10
  724.8 19.7 %custom-call.36 = f32[2,128,128]{1,2,0:T(8,128)S(1)} custom-call(f32[2,128,128]{2,1,0:T(8,128)S(1)} %get-tuple-element.90), custom_call_target="InvertDiagBlocksLowerTriangular" | custom-call | tf_op jit(solution)/shard_map/triangular_solve/custom-call.0 | solution.py:26
  745.5 56.0 %all-gather.51.cloned.1.call-done = f32[8192,1024]{1,0:T(8,128)} async-done(((f32[256,1024]{1,0:T(8,128)}), f32[8192,1024]{1,0:T(8,128)}) %all-gather.51.cloned.1.call-update) | async-done | bytes 33554448 | tf_op jit(solution)/shard_map/all_gather | solution.py:11
  801.5 11.8 %reduce_sum.113 = f32[256,1024]{1,0:T(8,128)S(1)} reduce(f32[32,256,1024]{2,1,0:T(8,128)} %bitcast.242, f32[]{:T(128)} %constant.178.clone.1), dimensions={0}, to_apply=%region_10.14 | reduce | flops 8126464 | bytes 34603012 | tf_op jit(solution)/shard_map/reduce_sum | solution.py:12
  813.4 1.5 fusion.17
  816.2 2.1 broadcast_select_fusion
  819.7 32.7 %all-gather.59.cloned.1.call-done = f32[32,65,256]{2,1,0:T(8,128)} async-done(((f32[1,65,256]{2,1,0:T(8,128)}), f32[32,65,256]{2,1,0:T(8,128)}) %all-gather.59.cloned.1.call-update) | async-done | bytes 2129936 | tf_op jit(solution)/shard_map/all_gather | solution.py:11
  852.4 1.8 reduce_sum.118
  855.9 39.7 %all-gather.53.cloned.1.call-done = f32[2048,256]{1,0:T(8,128)} async-done(((f32[256,256]{1,0:T(8,128)}), f32[2048,256]{1,0:T(8,128)}) %all-gather.53.cloned.1.call-update) | async-done | bytes 2097168 | tf_op jit(solution)/shard_map/all_gather | solution.py:17
  895.7 1.7 dynamic-slice_select_fusion
  900.1 45.4 %all-gather.61.cloned.1.call-done = f32[32,65,256]{2,1,0:T(8,128)} async-done(((f32[1,65,256]{2,1,0:T(8,128)}), f32[32,65,256]{2,1,0:T(8,128)}) %all-gather.61.cloned.1.call-update) | async-done | bytes 2129936 | tf_op jit(solution)/shard_map/all_gather | solution.py:11
  945.5 1.8 reduce_sum.119
  947.3 58.8 %all-gather.37.cloned.1.call-done = f32[32,256,256]{2,1,0:T(8,128)} async-done(((f32[1,256,256]{2,1,0:T(8,128)}), f32[32,256,256]{2,1,0:T(8,128)}) %all-gather.37.cloned.1.call-update) | async-done | bytes 8388624 | tf_op jit(solution)/shard_map/all_gather | solution.py:11
  1006.2 3.9 reduce_sum.114
  1010.3 11.7 %cholesky.316 = f32[128,128]{1,0:T(8,128)S(1)} custom-call(f32[128,128]{1,0:T(8,128)S(1)} %cholesky.355), custom_call_target="Cholesky" | custom-call | tf_op jit(solution)/shard_map/jit(cholesky)/cholesky | solution.py:69
  1022.1 9.8 custom-call.38
  1032.4 11.7 %cholesky.333 = f32[128,128]{1,0:T(8,128)S(1)} custom-call(f32[128,128]{1,0:T(8,128)S(1)} %convolution_subtract_fusion.16), custom_call_target="Cholesky" | custom-call | tf_op jit(solution)/shard_map/jit(cholesky)/cholesky | solution.py:69
  1046.9 4.2 while.27
  1047.7 1.4 bitcast_dynamic-update-slice_fusion.11
  1051.1 19.7 %custom-call.39 = f32[2,128,128]{1,2,0:T(8,128)S(1)} custom-call(f32[2,128,128]{2,1,0:T(8,128)S(1)} %get-tuple-element.92), custom_call_target="InvertDiagBlocksLowerTriangular" | custom-call | tf_op jit(solution)/shard_map/triangular_solve/custom-call.0 | solution.py:26
  1075.4 52.5 %all-gather.55.cloned.1.call-done = f32[8192,1024]{1,0:T(8,128)} async-done(((f32[256,1024]{1,0:T(8,128)}), f32[8192,1024]{1,0:T(8,128)}) %all-gather.55.cloned.1.call-update) | async-done | bytes 33554448 | tf_op jit(solution)/shard_map/all_gather | solution.py:11
  1127.9 11.8 %reduce_sum.115 = f32[256,1024]{1,0:T(8,128)S(1)} reduce(f32[32,256,1024]{2,1,0:T(8,128)} %bitcast.245, f32[]{:T(128)} %constant.178.clone.1), dimensions={0}, to_apply=%region_14.18 | reduce | flops 8126464 | bytes 34603012 | tf_op jit(solution)/shard_map/reduce_sum | solution.py:12
  1141.6 2.1 fusion.1
  (226 shorter events, 49.4 us)
Async XLA Ops:
  7.2 49.8 %copy-start = (f32[256,1024]{1,0:T(8,128)S(1)}, f32[256,1024]{1,0:T(8,128)}, u32[]{:S(2)}) copy-start(f32[256,1024]{1,0:T(8,128)} %param.11) | copy-start | bytes 3145732
  7.2 48.0 %all-gather.41.cloned.1.call-start = ((), (), s32[]{:S(2)}) async-start(), calls=%async_computation.5 | async-start | bytes 2359296 | tf_op jit(solution)/shard_map/all_gather | solution.py:17
  11.0 103.8 %all-gather.31.cloned.1.call-start = ((), (), s32[]{:S(2)}) async-start(), calls=%async_computation | async-start | bytes 8650752 | tf_op jit(solution)/shard_map/all_gather | solution.py:11
  56.9 179.8 %all-gather.43.cloned.1.call-start = ((), (), s32[]{:S(2)}) async-start(), calls=%async_computation.6 | async-start | bytes 34603008 | tf_op jit(solution)/shard_map/all_gather | solution.py:11
  58.0 235.8 %all-gather.45.cloned.1.call-start = ((), (), s32[]{:S(2)}) async-start(), calls=%async_computation.7 | async-start | bytes 2359296 | tf_op jit(solution)/shard_map/all_gather | solution.py:17
  159.2 90.0 %copy-start.3 = (f32[256,256]{1,0:T(8,128)}, f32[256,256]{1,0:T(8,128)S(1)}, u32[]{:S(2)}) copy-start(f32[256,256]{1,0:T(8,128)S(1)} %get-tuple-element.402) | copy-start | bytes 786436
  178.9 70.9 %copy-start.8 = (f32[2,128,128]{1,2,0:T(8,128)}, f32[2,128,128]{1,2,0:T(8,128)S(1)}, u32[]{:S(2)}) copy-start(f32[2,128,128]{1,2,0:T(8,128)S(1)} %custom-call.30) | copy-start | bytes 393220
  179.9 70.5 %copy-start.5 = (f32[256,128]{0,1:T(8,128)}, f32[256,128]{0,1:T(8,128)S(1)}, u32[]{:S(2)}) copy-start(f32[256,128]{0,1:T(8,128)S(1)} %fusion.65) | copy-start | bytes 393220
  252.4 43.7 %copy-start.17 = (f32[64,256]{1,0:T(8,128)S(1)}, f32[64,256]{1,0:T(8,128)}, u32[]{:S(2)}) copy-start(f32[64,256]{1,0:T(8,128)} %param.14) | copy-start | bytes 196612
  252.5 43.7 %copy-start.20 = (f32[256]{0:T(256)S(1)}, f32[256]{0:T(256)}, u32[]{:S(2)}) copy-start(f32[256]{0:T(256)} %param.13) | copy-start | bytes 3076
  253.2 100.0 %all-gather.33.cloned.1.call-start = ((), (), s32[]{:S(2)}) async-start(), calls=%async_computation.1 | async-start | bytes 8650752 | tf_op jit(solution)/shard_map/all_gather | solution.py:11
  295.5 179.4 %all-gather.47.cloned.1.call-start = ((), (), s32[]{:S(2)}) async-start(), calls=%async_computation.8 | async-start | bytes 34603008 | tf_op jit(solution)/shard_map/all_gather | solution.py:11
  296.1 229.7 %all-gather.39.cloned.1.call-start = ((), (), s32[]{:S(2)}) async-start(), calls=%async_computation.4 | async-start | bytes 2433024 | tf_op jit(solution)/shard_map/all_gather | solution.py:11
  296.8 272.3 %all-gather.49.cloned.1.call-start = ((), (), s32[]{:S(2)}) async-start(), calls=%async_computation.9 | async-start | bytes 2359296 | tf_op jit(solution)/shard_map/all_gather | solution.py:17
  397.9 88.8 %copy-start.23 = (s32[2,2]{1,0:T(2,128)}, s32[2,2]{1,0:T(2,128)S(1)}, u32[]{:S(2)}) copy-start(s32[2,2]{1,0:T(2,128)S(1)} %get-tuple-element.439) | copy-start | bytes 52
  397.9 89.5 %copy-start.4 = (f32[256,256]{1,0:T(8,128)}, f32[256,256]{1,0:T(8,128)S(1)}, u32[]{:S(2)}) copy-start(f32[256,256]{1,0:T(8,128)S(1)} %get-tuple-element.403) | copy-start | bytes 786436
  417.6 70.4 %copy-start.10 = (f32[2,128,128]{1,2,0:T(8,128)}, f32[2,128,128]{1,2,0:T(8,128)S(1)}, u32[]{:S(2)}) copy-start(f32[2,128,128]{1,2,0:T(8,128)S(1)} %custom-call.33) | copy-start | bytes 393220
  490.6 37.0 %copy-start.9 = (f32[2,128,128]{1,2,0:T(8,128)S(1)}, f32[2,128,128]{1,2,0:T(8,128)}, u32[]{:S(2)}) copy-start(f32[2,128,128]{1,2,0:T(8,128)} %copy-done.8) | copy-start | bytes 393220
  490.6 38.5 %copy-start.6 = (f32[256,128]{0,1:T(8,128)S(1)}, f32[256,128]{0,1:T(8,128)}, u32[]{:S(2)}) copy-start(f32[256,128]{0,1:T(8,128)} %copy-done.5) | copy-start | bytes 393220
  490.6 38.6 %copy-start.18 = (f32[64,256]{1,0:T(8,128)S(1)}, f32[64,256]{1,0:T(8,128)}, u32[]{:S(2)}) copy-start(f32[64,256]{1,0:T(8,128)} %param.14) | copy-start | bytes 196612
  491.4 127.7 %all-gather.57.cloned.1.call-start = ((), (), s32[]{:S(2)}) async-start(), calls=%async_computation.13 | async-start | bytes 2433024 | tf_op jit(solution)/shard_map/all_gather | solution.py:11
  492.0 80.3 %copy-start.19 = (s32[4]{0:T(128)S(1)}, s32[4]{0:T(128)}, u32[]{:S(2)}) copy-start(s32[4]{0:T(128)} %param.12) | copy-start | bytes 52
  530.1 90.8 %copy-start.11 = (f32[2,128,128]{1,2,0:T(8,128)S(1)}, f32[2,128,128]{1,2,0:T(8,128)}, u32[]{:S(2)}) copy-start(f32[2,128,128]{1,2,0:T(8,128)} %copy-done.10) | copy-start | bytes 393220
  530.1 149.6 %all-gather.35.cloned.1.call-start = ((), (), s32[]{:S(2)}) async-start(), calls=%async_computation.2 | async-start | bytes 8650752 | tf_op jit(solution)/shard_map/all_gather | solution.py:11
  570.8 230.8 %all-gather.51.cloned.1.call-start = ((), (), s32[]{:S(2)}) async-start(), calls=%async_computation.10 | async-start | bytes 34603008 | tf_op jit(solution)/shard_map/all_gather | solution.py:11
  571.5 280.9 %all-gather.59.cloned.1.call-start = ((), (), s32[]{:S(2)}) async-start(), calls=%async_computation.14 | async-start | bytes 2433024 | tf_op jit(solution)/shard_map/all_gather | solution.py:11
  622.7 61.0 %copy-start.15 = (f32[65,256]{1,0:T(8,128)}, f32[65,256]{1,0:T(8,128)S(1)}, u32[]{:S(2)}) copy-start(f32[65,256]{1,0:T(8,128)S(1)} %fusion.4) | copy-start | bytes 199684
  623.4 272.2 %all-gather.53.cloned.1.call-start = ((), (), s32[]{:S(2)}) async-start(), calls=%async_computation.11 | async-start | bytes 2359296 | tf_op jit(solution)/shard_map/all_gather | solution.py:17
  683.7 36.8 %copy-start.24 = (s32[2,2]{1,0:T(2,128)S(1)}, s32[2,2]{1,0:T(2,128)}, u32[]{:S(2)}) copy-start(s32[2,2]{1,0:T(2,128)} %copy-done.23) | copy-start | bytes 52
  744.4 57.1 %copy-start.12 = (f32[2,128,128]{1,2,0:T(8,128)}, f32[2,128,128]{1,2,0:T(8,128)S(1)}, u32[]{:S(2)}) copy-start(f32[2,128,128]{1,2,0:T(8,128)S(1)} %custom-call.36) | copy-start | bytes 393220
  745.5 109.4 %copy-start.1 = (f32[256,256]{0,1:T(8,128)}, f32[256,256]{0,1:T(8,128)S(1)}, u32[]{:S(2)}) copy-start(f32[256,256]{0,1:T(8,128)S(1)} %maximum_multiply_fusion.7) | copy-start | bytes 786436
  813.4 2.1 copy-start.13
  818.2 36.0 %copy-start.14 = (f32[2,128,128]{1,2,0:T(8,128)S(1)}, f32[2,128,128]{1,2,0:T(8,128)}, u32[]{:S(2)}) copy-start(f32[2,128,128]{1,2,0:T(8,128)} %copy-done.12) | copy-start | bytes 393220
  818.2 36.7 %copy-start.16 = (f32[65,256]{1,0:T(8,128)S(1)}, f32[65,256]{1,0:T(8,128)}, u32[]{:S(2)}) copy-start(f32[65,256]{1,0:T(8,128)} %copy-done.15) | copy-start | bytes 199684
  819.0 126.5 %all-gather.61.cloned.1.call-start = ((), (), s32[]{:S(2)}) async-start(), calls=%async_computation.15 | async-start | bytes 2433024 | tf_op jit(solution)/shard_map/all_gather | solution.py:11
  855.9 150.3 %all-gather.37.cloned.1.call-start = ((), (), s32[]{:S(2)}) async-start(), calls=%async_computation.3 | async-start | bytes 8650752 | tf_op jit(solution)/shard_map/all_gather | solution.py:11
  897.4 230.5 %all-gather.55.cloned.1.call-start = ((), (), s32[]{:S(2)}) async-start(), calls=%async_computation.12 | async-start | bytes 34603008 | tf_op jit(solution)/shard_map/all_gather | solution.py:11
  1010.1 36.8 %copy-start.25 = (s32[2,2]{1,0:T(2,128)S(1)}, s32[2,2]{1,0:T(2,128)}, u32[]{:S(2)}) copy-start(s32[2,2]{1,0:T(2,128)} %copy-done.23) | copy-start | bytes 52
  1010.3 62.2 %copy-start.21 = (f32[256]{0:T(256)S(1)}, f32[256]{0:T(256)}, u32[]{:S(2)}) copy-start(f32[256]{0:T(256)} %convert_element_type.60) | copy-start | bytes 3076
  1022.0 50.5 %copy-start.22 = (pred[256]{0:T(512)(128)(4,1)S(1)}, pred[256]{0:T(512)(128)(4,1)}, u32[]{:S(2)}) copy-start(pred[256]{0:T(512)(128)(4,1)} %broadcast_compare_fusion.2) | copy-start | bytes 772
  1032.1 41.9 %copy-start.2 = (f32[256,256]{0,1:T(8,128)S(1)}, f32[256,256]{0,1:T(8,128)}, u32[]{:S(2)}) copy-start(f32[256,256]{0,1:T(8,128)} %copy-done.1) | copy-start | bytes 786436
  1032.2 41.9 %copy-start.7 = (f32[256,128]{0,1:T(8,128)S(1)}, f32[256,128]{0,1:T(8,128)}, u32[]{:S(2)}) copy-start(f32[256,128]{0,1:T(8,128)} %copy-done.5) | copy-start | bytes 393220
Sparse Core Ops, SparseCore 0:
  11.1 44.0 all-gather.40
  58.3 56.4 all-gather.30
  117.9 118.7 all-gather.42
  253.3 40.3 all-gather.44
  296.7 56.4 all-gather.32
  356.2 118.5 all-gather.46
  477.4 48.3 all-gather.38
  528.2 40.8 all-gather.48
  571.6 47.4 all-gather.56
  622.1 57.6 all-gather.34
  682.9 118.6 all-gather.50
  803.9 48.4 all-gather.58
  854.8 40.8 all-gather.52
  898.0 47.4 all-gather.60
  948.5 57.6 all-gather.36
  1009.2 118.6 all-gather.54
